TPU v7x, 512 devices: a whole 4x8x8 slice. The times are simulated.
512 devices in a mesh: segment: 16 (over y, z_lo), ctx: 32 (over x, z_hi, core).
Axes of the slice: x: 4, y: 8, z: 8 (z_hi: 4, z_lo: 2; z = z_hi * 2 + z_lo), core: 2. Of those that a mesh axis runs over, the one named last changes fastest.
Arguments:
- perturbed_frame_activation: bfloat16 [2, 256, 1536], P(None, 'ctx'), may hold values from -8 to 8
- inbound_activation: bfloat16 [16, 256, 1536], P('segment', 'ctx'), may hold values from -6 to 6
- section_block_indices: int32 [16], P('segment'), may hold values from 1 to 2, as said below
- tile_arrival_permutation: int32 [2], replicated, may hold values from 0 to 1, each once
- adaptive_shifting: float32 [16, 2, 1536], P('segment'), may hold values from -6 to 6
- adaptive_scaling: float32 [16, 2, 1536], P('segment'), may hold values from -4 to 4
- tier_query_factor: float32 [16, 2, 1536], P('segment'), may hold values from 0.3 to 3
- tier_skip_coefficient: float32 [16, 2, 1536], P('segment'), may hold values from -12 to 12
- earlier_step_lookup_matrix: bfloat16 [16, 2, 2, 256, 1536], P('segment', None, None, 'ctx'), may hold values from -10.5 to 10.5
- earlier_step_content_matrix: bfloat16 [16, 2, 2, 256, 1536], P('segment', None, None, 'ctx'), may hold values from -3 to 3
Outputs:
- section_out: bfloat16 [16, 2, 256, 1536], P('segment', None, 'ctx')
Inputs may be any that keep to these rules, and one draw needn't show every extreme that they name: `section_block_indices`: some segment uses exactly 2 slots and some exactly 1. `tile_arrival_permutation`: each patch once.
All inputs are finite; a program needn't handle non-finite values.
Results may differ from a plain program's by a relative error of at most 0.013.
Values may be sent and summed in bfloat16 or wider, within the bound.
No kernel may reach another device: no remote copies, remote signals or barrier semaphores. Data moves between devices by JAX's collectives and lax.ppermute only.
A program may use at most 64 MiB of HBM per device.

v0:
```python
import math
import jax
import jax.numpy as jnp
from jax import lax
from jax.sharding import PartitionSpec as P

HD = 128
EPSILON = 1e-06


def head_norm(values):
    return values * lax.rsqrt(jnp.mean(values * values, axis=-1, keepdims=True) + EPSILON)


def per_device(
    perturbed_frame_activation,
    inbound_activation,
    section_block_indices,
    tile_arrival_permutation,
    adaptive_shifting,
    adaptive_scaling,
    tier_query_factor,
    tier_skip_coefficient,
    earlier_step_lookup_matrix,
    earlier_step_content_matrix,
):
    segment = lax.axis_index("segment")
    place = lax.axis_index("ctx")
    patch_count = tile_arrival_permutation.shape[0]
    rows = inbound_activation.shape[1]
    width = inbound_activation.shape[2]
    heads = width // HD
    slot_count = earlier_step_lookup_matrix.shape[1]
    layers_here = section_block_indices[0]
    scale = 1.0 / math.sqrt(HD)

    def pick_patch(stack, patch, axis):
        return lax.dynamic_index_in_dim(stack, patch, axis, keepdims=False)

    first_rows = jnp.where(
        segment == 0,
        pick_patch(perturbed_frame_activation, tile_arrival_permutation[0], 0),
        inbound_activation[0],
    )
    entry_rows = [first_rows[None]]
    for turn in range(1, patch_count):
        entry_rows.append(
            pick_patch(perturbed_frame_activation, tile_arrival_permutation[turn], 0)[None]
        )
    other_patch = tile_arrival_permutation[jnp.mod(1 - segment, patch_count)]
    far_k = pick_patch(earlier_step_lookup_matrix[0], other_patch, 1)
    far_v = pick_patch(earlier_step_content_matrix[0], other_patch, 1)
    packed = jnp.concatenate(entry_rows + [far_k, far_v], axis=0)
    whole = lax.all_gather(packed, "ctx", axis=1, tiled=True)
    entry = whole[:patch_count]
    far_k = whole[patch_count : patch_count + slot_count]
    far_v = whole[patch_count + slot_count :]
    tokens = whole.shape[1]

    def layer(state, tier, keys_far, values_far):
        live = layers_here > tier
        x = state.astype(jnp.float32)
        hidden = (
            x
            * lax.rsqrt(jnp.mean(x * x, axis=-1, keepdims=True) + EPSILON)
            * (1.0 + adaptive_scaling[0, tier])
            + adaptive_shifting[0, tier]
        )
        query = head_norm(hidden.reshape(tokens, heads, HD)).astype(jnp.bfloat16)
        fresh_key = head_norm(
            (hidden * tier_query_factor[0, tier]).reshape(tokens, heads, HD)
        ).astype(jnp.bfloat16)
        fresh_value = hidden.astype(jnp.bfloat16).reshape(tokens, heads, HD)
        keys = jnp.concatenate([fresh_key, keys_far.reshape(tokens, heads, HD)], axis=0)
        values = jnp.concatenate([fresh_value, values_far.reshape(tokens, heads, HD)], axis=0)
        scores = jnp.einsum("phd,nhd->phn", query, keys, preferred_element_type=jnp.float32) * scale
        weights = jnp.exp(scores)
        total = jnp.sum(weights, axis=-1)
        numerator = jnp.einsum(
            "phn,nhd->phd", weights.astype(jnp.bfloat16), values, preferred_element_type=jnp.float32
        )
        attended = (numerator / total[..., None]).reshape(tokens, width)
        new_state = (x + tier_skip_coefficient[0, tier] * attended).astype(jnp.bfloat16)
        return (
            jnp.where(live, new_state, state),
            fresh_key.reshape(tokens, width),
            fresh_value.reshape(tokens, width),
        )

    def own_rows(state):
        return lax.dynamic_slice_in_dim(state, place * rows, rows, 0)

    outcomes = []
    state = entry[0]
    turn_zero_kv = []
    for tier in range(slot_count):
        state, fresh_key, fresh_value = layer(state, tier, far_k[tier], far_v[tier])
        turn_zero_kv.append((fresh_key, fresh_value))
    outcomes.append(own_rows(state))
    count = lax.axis_size("segment")
    for turn in range(1, patch_count):
        arrived = lax.ppermute(state, "segment", [(i, i + 1) for i in range(count - 1)])
        state = jnp.where(segment == 0, entry[turn], arrived)
        for tier in range(slot_count):
            state, _, _ = layer(state, tier, *turn_zero_kv[tier])
        outcomes.append(own_rows(state))
    return jnp.stack(outcomes)[None]


def solution(mesh):
    return jax.shard_map(
        per_device,
        mesh=mesh,
        in_specs=(
            P(None, "ctx", None),
            P("segment", "ctx", None),
            P("segment"),
            P(),
            P("segment", None, None),
            P("segment", None, None),
            P("segment", None, None),
            P("segment", None, None),
            P("segment", None, None, "ctx", None),
            P("segment", None, None, "ctx", None),
        ),
        out_specs=P("segment", None, "ctx", None),
        check_vma=False,
    )
```

profile of v0, /device:TPU:32, one launch (start us, length us, event | category | flops | bytes accessed | tf_op | source)
XLA Modules:
  0.0 188.3 jit_solution(44315173992806719)
XLA Ops:
  6.5 1.4 fusion.106
  19.1 70.0 %all-gather.2.cloned.1.call-done = bf16[6,256,1536]{2,1,0:T(8,128)(2,1)} async-done(((bf16[6,8,1536]{2,1,0:T(8,128)(2,1)}), bf16[6,256,1536]{2,1,0:T(8,128)(2,1)}) %all-gather.2.cloned.1.call-update) | async-done | bytes 4718608 | tf_op jit(solution)/shard_map/all_gather | solution.py:54
  89.1 1.4 fusion.8
  90.5 3.5 %fusion.105 = (bf16[1,256,1536]{2,1,0:T(8,128)(2,1)}, bf16[1,256,1536]{2,1,0:T(8,128)(2,1)}, bf16[1,256,1536]{2,1,0:T(8,128)(2,1)S(1)}, bf16[1,256,1536]{2,1,0:T(8,128)(2,1)S(1)}, bf16[1,256,1536]{2,1,0:T(8,128)(2,1)S(1)}) fusion(bf16[6,256,1536]{2,1,0:T(8,128)(2,1)} %all-gather.2.cloned.1.call-done), kind=kLoop, calls=%fused_computation.164 | loop fusion | bytes 7864320 | tf_op jit(solution)/shard_map/slice | solution.py:97
  94.0 1.4 copy.38
  96.6 1.4 copy.40
  103.6 1.5 bitcast_reduce_fusion.3
  105.1 2.0 %bitcast_divide_fusion.3 = f32[256,12,128]{2,0,1:T(8,128)S(1)} fusion(f32[12,512,256]{2,1,0:T(8,128)S(1)} %get-tuple-element.43, bf16[256,12,128]{2,0,1:T(8,128)(2,1)S(1)} %copy.29, bf16[256,12,128]{2,0,1:T(8,128)(2,1)S(1)} %get-tuple-element.36, f32[256,12]{0,1:T(8,128)S(1)} %get-tuple-element.42), kind=kOutput, calls=%fused_computation.81 | convolution fusion | flops 409337856 | bytes 9449472 | tf_op jit(solution)/shard_map/phn,nhd->phd/dot_general | solution.py:79
  107.1 1.6 copy.35
  108.7 3.0 %copy.36 = f32[256,1536]{1,0:T(8,128)} copy(f32[256,1536]{0,1:T(8,128)} %bitcast.90) | data formatting | bytes 3145728 | tf_op jit(solution)/shard_map/reshape | solution.py:82
  111.7 2.0 %fusion.23 = (f32[256]{0:T(256)S(1)}, bf16[256,1536]{1,0:T(8,128)(2,1)S(1)}) fusion(f32[256,1536]{1,0:T(8,128)} %copy.36, f32[1536]{0:T(1024)S(1)} %get-tuple-element.10, bf16[6,256,1536]{2,1,0:T(8,128)(2,1)} %all-gather.2.cloned.1.call-done, pred[]{:T(512)} %bitcast.1), kind=kLoop, calls=%fused_computation.44 | loop fusion | flops 3145472 | bytes 3152897 | tf_op jit(solution)/shard_map/reduce_sum | solution.py:65
  115.9 1.4 bitcast_reduce_fusion.2
  117.3 2.3 %bitcast_divide_fusion.2 = f32[256,12,128]{0,2,1:T(8,128)} fusion(f32[12,512,256]{2,1,0:T(8,128)S(1)} %get-tuple-element.45, bf16[256,12,128]{2,0,1:T(8,128)(2,1)S(1)} %copy-done.6, bf16[256,12,128]{2,0,1:T(8,128)(2,1)S(1)} %get-tuple-element.21, f32[256,12]{0,1:T(8,128)S(1)} %get-tuple-element.44), kind=kOutput, calls=%fused_computation.80 | convolution fusion | flops 409337856 | bytes 9449472 | tf_op jit(solution)/shard_map/phn,nhd->phd/dot_general | solution.py:79
  119.7 1.9 copy.44
  121.8 2.8 %collective-permute-start = (bf16[256,1536]{1,0:T(8,128)(2,1)S(1)}, bf16[256,1536]{1,0:T(8,128)(2,1)S(1)}, u32[]{:S(2)}, u32[]{:S(2)}) collective-permute-start(bf16[256,1536]{1,0:T(8,128)(2,1)S(1)} %fusion.68), channel_id=1, source_target_pairs={{0,32},{32,64},{64,96},{96,128},{128,160},{160,192},{192,224},{224... | collective-permute-start | bytes 2359304 | tf_op jit(solution)/shard_map/ppermute | solution.py:102
  124.6 20.9 %collective-permute-done = bf16[256,1536]{1,0:T(8,128)(2,1)S(1)} collective-permute-done((bf16[256,1536]{1,0:T(8,128)(2,1)S(1)}, bf16[256,1536]{1,0:T(8,128)(2,1)S(1)}, u32[]{:S(2)}, u32[]{:S(2)}) %collective-permute-start) | collective-permute-done | bytes 786464 | tf_op jit(solution)/shard_map/ppermute | solution.py:102
  145.5 1.5 fusion.25
  147.0 2.2 %fusion.99 = (bf16[256,1536]{1,0:T(8,128)(2,1)}, f32[256,1536]{1,0:T(8,128)}, f32[256,1536]{1,0:T(8,128)}) fusion(f32[1536]{0:T(1024)S(1)} %get-tuple-element.52, f32[1536]{0:T(1024)S(1)} %get-tuple-element.12, f32[256]{0:T(256)S(1)} %add_rsqrt_fusion.9, bf16[256,1536]{1,0:T(8,128)(2,1)S(1)} %get-tuple-element.20, f32[1536]{0:T(1024)S(1)} %get-tuple-element.16), kind=kLoop, calls=%fused_computation.162 | loop fusion | flops 2359296 | bytes 4738048 | tf_op jit(solution)/shard_map/convert_element_type | solution.py:73
  149.3 1.9 copy.47
  151.3 1.6 copy.48
  152.9 1.4 copy.45
  155.5 1.9 copy.49
  159.3 1.5 bitcast_reduce_fusion.1
  160.8 2.3 %bitcast_divide_fusion.1 = f32[256,12,128]{0,2,1:T(8,128)} fusion(f32[12,512,256]{2,1,0:T(8,128)S(1)} %get-tuple-element.47, bf16[256,12,128]{2,0,1:T(8,128)(2,1)S(1)} %copy-done.13, bf16[256,12,128]{2,0,1:T(8,128)(2,1)S(1)} %copy-done.9, f32[256,12]{0,1:T(8,128)S(1)} %get-tuple-element.46), kind=kOutput, calls=%fused_computation.79 | convolution fusion | flops 409337856 | bytes 9449472 | tf_op jit(solution)/shard_map/phn,nhd->phd/dot_general | solution.py:79
  163.1 1.9 copy.53
  165.0 1.4 fusion.100
  166.7 2.0 %fusion.98 = (bf16[256,1536]{1,0:T(8,128)(2,1)S(1)}, f32[256,1536]{1,0:T(8,128)}, f32[256,1536]{1,0:T(8,128)}) fusion(f32[1536]{0:T(1024)S(1)} %get-tuple-element.53, f32[1536]{0:T(1024)S(1)} %get-tuple-element.11, f32[256]{0:T(256)S(1)} %add_rsqrt_fusion.8, bf16[256,1536]{1,0:T(8,128)(2,1)S(1)} %get-tuple-element.18, f32[1536]{0:T(1024)S(1)} %get-tuple-element.15), kind=kLoop, calls=%fused_computation.161 | loop fusion | flops 2359296 | bytes 4738048 | tf_op jit(solution)/shard_map/convert_element_type | solution.py:73
  168.7 1.9 copy.56
  170.7 1.6 copy.57
  173.0 1.9 copy.58
  176.8 1.3 bitcast_reduce_fusion
  178.1 1.4 bitcast_divide_fusion
  (77 shorter events, 21.9 us)
Async XLA Ops:
  6.5 82.6 %all-gather.2.cloned.1.call-start = ((), (), s32[]{:S(2)}) async-start(), calls=%async_computation | async-start | bytes 4866048 | tf_op jit(solution)/shard_map/all_gather | solution.py:54
  102.0 1.6 copy-start.8
  103.0 2.1 %copy-start.12 = (bf16[256,12,128]{2,0,1:T(8,128)(2,1)}, bf16[256,12,128]{2,0,1:T(8,128)(2,1)S(1)}, u32[]{:S(2)}) copy-start(bf16[256,12,128]{2,0,1:T(8,128)(2,1)S(1)} %get-tuple-element.36) | copy-start | bytes 2359300
  103.6 1.5 copy-start.4
  114.3 3.0 %copy-start.10 = (bf16[256,12,128]{2,0,1:T(8,128)(2,1)}, bf16[256,12,128]{2,0,1:T(8,128)(2,1)S(1)}, u32[]{:S(2)}) copy-start(bf16[256,12,128]{2,0,1:T(8,128)(2,1)S(1)} %get-tuple-element.21) | copy-start | bytes 2359300
  114.3 1.6 copy-start.7
  115.9 1.4 copy-start.2
  115.9 1.4 copy-start.6
  121.8 23.7 %collective-permute-start = (bf16[256,1536]{1,0:T(8,128)(2,1)S(1)}, bf16[256,1536]{1,0:T(8,128)(2,1)S(1)}, u32[]{:S(2)}, u32[]{:S(2)}) collective-permute-start(bf16[256,1536]{1,0:T(8,128)(2,1)S(1)} %fusion.68), channel_id=1, source_target_pairs={{0,32},{32,64},{64,96},{96,128},{128,160},{160,192},{192,224},{224... | collective-permute-start | bytes 2359304 | tf_op jit(solution)/shard_map/ppermute | solution.py:102
  157.4 1.4 copy-start
  157.5 1.7 copy-start.5
  159.3 1.5 copy-start.9
  159.3 1.5 copy-start.13
  174.9 1.4 copy-start.1
  175.0 1.7 copy-start.3
  176.8 1.3 copy-start.11
Sparse Core Ops, SparseCore 0:
  16.1 72.9 all-gather.1
where the time goes:
time: 189 us; the launch traced here: 188 us
  waiting for transfers between devices  90.9 us (48%)
  local copies, waits for them, and re-layouts  40.8 us (22%)
  between operations  20.3 us (11%)
  other arithmetic  19.9 us (11%)
  matrix products  13.6 us (7%)
  starting transfers between devices  2.77 us (1%)
    all_gather x1, waiting for transfers between devices, per_device(): whole = lax.all_gather(packed, 'ctx', axis=1, tiled=True)  70 us
    ppermute x1, waiting for transfers between devices, per_device(): lax.ppermute(state, 'segment', [(i, i + 1) for i in range(count - 1)])  20.9 us
    dot_general x4, matrix products, layer(): jnp.einsum('phn,nhd->phd', weights.astype(jnp.bfloat16), values, preferre...  7.99 us
    slice x5, local copies, waits for them, and re-layouts, per_device(): state, fresh_key, fresh_value = layer(state, tier, far_k[tier], far_v[tier])  6.85 us
    reshape x3, local copies, waits for them, and re-layouts, layer(): attended = (numerator / total[..., None]).reshape(tokens, width)  6.77 us
    dot_general x4, matrix products, layer(): jnp.einsum('phd,nhd->phn', query, keys, preferred_element_type=jnp.float32)  5.65 us
    reduce_sum x4, other arithmetic, layer(): jnp.mean(x * x, axis=-1, keepdims=True) + EPSILON  5.12 us
    convert_element_type x3, other arithmetic, layer(): fresh_value = hidden.astype(jnp.bfloat16).reshape(tokens, heads, HD)  4.79 us
  transfers between devices with their start and end apart: 2, of which 2 were waited for; matrix products, arithmetic and copies ran while one was open for 1% of the time, Pallas kernels for 0%

commit v1 on v0

--- a/solution.py
+++ b/solution.py
@@ -51,7 +51,9 @@
     far_k = pick_patch(earlier_step_lookup_matrix[0], other_patch, 1)
     far_v = pick_patch(earlier_step_content_matrix[0], other_patch, 1)
     packed = jnp.concatenate(entry_rows + [far_k, far_v], axis=0)
-    whole = lax.all_gather(packed, "ctx", axis=1, tiled=True)
+    whole = jnp.concatenate(
+        lax.all_to_all(jnp.stack([packed] * lax.axis_size("ctx")), "ctx", 0, 0), axis=1
+    )
     entry = whole[:patch_count]
     far_k = whole[patch_count : patch_count + slot_count]
     far_v = whole[patch_count + slot_count :]

time: 189 us -> 241 us (1.28)
  the two profiles are of different devices: /device:TPU:32 before, /device:TPU:41 now
where the time goes in v1:
time: 241 us; the launch traced here: 240 us
  waiting for transfers between devices  101 us (42%)
  local copies, waits for them, and re-layouts  56.3 us (23%)
  starting transfers between devices  42.2 us (18%)
  other arithmetic  20 us (8%)
  matrix products  13.4 us (6%)
  between operations  6.92 us (3%)
    all_to_all x1, waiting for transfers between devices, per_device(): lax.all_to_all(jnp.stack([packed] * lax.axis_size('ctx')), 'ctx', 0, 0)  83.1 us
    ppermute x1, starting transfers between devices, per_device(): lax.ppermute(state, 'segment', [(i, i + 1) for i in range(count - 1)])  28.4 us
    ppermute x1, waiting for transfers between devices, per_device(): lax.ppermute(state, 'segment', [(i, i + 1) for i in range(count - 1)])  18.1 us
    all_to_all x1, starting transfers between devices, per_device(): lax.all_to_all(jnp.stack([packed] * lax.axis_size('ctx')), 'ctx', 0, 0)  13.8 us
    reshape x4, local copies, waits for them, and re-layouts, layer(): attended = (numerator / total[..., None]).reshape(tokens, width)  9.56 us
    dot_general x4, matrix products, layer(): jnp.einsum('phn,nhd->phd', weights.astype(jnp.bfloat16), values, preferre...  7.8 us
    another operation x4, local copies, waits for them, and re-layouts, layer(): values_far.reshape(tokens, heads, HD)  6.66 us
    another operation x4, local copies, waits for them, and re-layouts, layer(): keys_far.reshape(tokens, heads, HD)  6.1 us
  transfers between devices with their start and end apart: 2, of which 2 were waited for; matrix products, arithmetic and copies ran while one was open for 0% of the time, Pallas kernels for 0%

profile of v1, /device:TPU:41, one launch (start us, length us, event | category | flops | bytes accessed | tf_op | source)
XLA Modules:
  0.0 240.0 jit_solution(11342831954980718103)
XLA Ops:
  8.8 2.7 %stack.8 = bf16[32,6,8,1536]{3,2,1,0:T(8,128)(2,1)} broadcast(bf16[6,8,1536]{2,1,0:T(8,128)(2,1)S(1)} %pad_maximum_fusion), dimensions={1,2,3} | broadcast | bytes 4866048 | tf_op jit(solution)/shard_map/stack | solution.py:55
  11.5 13.8 %all-to-all-start = ((bf16[32,6,8,1536]{3,2,1,0:T(8,128)(2,1)}), bf16[32,6,8,1536]{3,2,1,0:T(8,128)(2,1)}, u32[]{:S(2)}, u32[]{:S(2)}) async-start(bf16[32,6,8,1536]{3,2,1,0:T(8,128)(2,1)} %stack.8), calls=%async_computation | async-start | bytes 9437184 | tf_op jit(solution)/shard_map/all_to_all | solution.py:55
  26.1 83.1 %all-to-all-done = bf16[32,6,8,1536]{3,2,1,0:T(8,128)(2,1)} async-done(((bf16[32,6,8,1536]{3,2,1,0:T(8,128)(2,1)}), bf16[32,6,8,1536]{3,2,1,0:T(8,128)(2,1)}, u32[]{:S(2)}, u32[]{:S(2)}) %all-to-all-start) | async-done | bytes 4718624 | tf_op jit(solution)/shard_map/all_to_all | solution.py:55
  109.2 2.7 %copy.122 = bf16[32,6,8,1536]{3,2,0,1:T(8,128)(2,1)S(1)} copy(bf16[32,6,8,1536]{3,2,1,0:T(8,128)(2,1)} %all-to-all-done) | data formatting | bytes 9437184 | tf_op jit(solution)/shard_map/all_to_all | solution.py:55
  112.2 2.0 fusion.104
  117.6 1.9 reshape_squeeze.13
  120.7 1.6 reshape_squeeze.12
  124.9 1.8 bitcast_divide_fusion.3
  126.7 1.6 copy.68
  128.3 2.3 copy.71
  130.7 2.5 %reshape_squeeze.14 = bf16[256,12,128]{2,1,0:T(8,128)(2,1)} reshape(bf16[1,32,8,1536]{3,2,1,0:T(8,128)(2,1)} %get-tuple-element.23) | data formatting | bytes 1572864 | tf_op jit(solution)/shard_map/reshape;squeeze | solution.py:77
  133.2 2.3 copy.72
  135.5 1.6 reshape_squeeze.15
  138.5 3.1 %copy.69 = f32[256,1536]{1,0:T(8,128)} copy(f32[256,1536]{0,1:T(8,128)} %bitcast.101) | data formatting | bytes 3145728 | tf_op jit(solution)/shard_map/reshape | solution.py:84
  141.6 2.6 %reshape.370 = f32[1,32,8,1536]{3,2,1,0:T(8,128)} reshape(f32[256,12,128]{2,1,0:T(8,128)} %copy.71) | data formatting | bytes 3145728 | tf_op jit(solution)/shard_map/reshape | solution.py:84
  144.2 2.0 multiply_reduce_fusion.7
  149.9 2.3 bitcast_divide_fusion.2
  152.2 2.0 copy.76
  154.3 2.5 %fusion.66 = bf16[256,1536]{1,0:T(8,128)(2,1)} fusion(f32[256,1536]{1,0:T(8,128)S(1)} %copy.76, f32[256,1536]{1,0:T(8,128)S(1)} %copy-done.3, f32[1536]{0:T(1024)S(1)} %get-tuple-element.9, f32[1536]{0:T(1024)S(1)} %get-tuple-element.10, pred[]{:T(512)} %bitcast.1, pred[]{:T(512)} %bitcast, bf16[6,32,8,1536]{3,2,1,0:T(8,128)(2,1)} %bitcast.91), kind=kLoop, calls=%fused_computation.100 | loop fusion | flops 3932160 | bytes 4730882 | tf_op jit(solution)/shard_map/jit(_where)/select_n | solution.py:87
  156.7 28.4 %collective-permute-start = (bf16[256,1536]{1,0:T(8,128)(2,1)}, bf16[256,1536]{1,0:T(8,128)(2,1)S(1)}, u32[]{:S(2)}, u32[]{:S(2)}) collective-permute-start(bf16[256,1536]{1,0:T(8,128)(2,1)} %fusion.66), channel_id=1, source_target_pairs={{0,32},{32,64},{64,96},{96,128},{128,160},{160,192},{192,224},{224... | collective-permute-start | bytes 2359304 | tf_op jit(solution)/shard_map/ppermute | solution.py:104
  185.9 18.1 %collective-permute-done = bf16[256,1536]{1,0:T(8,128)(2,1)S(1)} collective-permute-done((bf16[256,1536]{1,0:T(8,128)(2,1)}, bf16[256,1536]{1,0:T(8,128)(2,1)S(1)}, u32[]{:S(2)}, u32[]{:S(2)}) %collective-permute-start) | collective-permute-done | bytes 786464 | tf_op jit(solution)/shard_map/ppermute | solution.py:104
  205.5 2.4 fusion.99
  207.8 1.9 copy.79
  209.8 1.6 copy.80
  214.1 1.9 copy.81
  217.9 1.5 bitcast_reduce_fusion.1
  219.4 2.3 bitcast_divide_fusion.1
  221.7 1.9 copy.85
  225.3 2.0 fusion.98
  227.3 1.9 copy.88
  229.3 1.6 copy.89
  231.6 1.9 copy.90
  (93 shorter events, 31.4 us)
Async XLA Ops:
  11.5 14.5 %copy-start.16 = (f32[1,2,1536]{2,1,0:T(2,128)S(1)}, f32[1,2,1536]{2,1,0:T(2,128)}, u32[]{:S(2)}) copy-start(f32[1,2,1536]{2,1,0:T(2,128)} %param.17) | copy-start | bytes 36868
  11.5 14.5 %copy-start.17 = (f32[1,2,1536]{2,1,0:T(2,128)S(1)}, f32[1,2,1536]{2,1,0:T(2,128)}, u32[]{:S(2)}) copy-start(f32[1,2,1536]{2,1,0:T(2,128)} %param.15) | copy-start | bytes 36868
  11.5 14.6 %copy-start.18 = (f32[1,2,1536]{2,1,0:T(2,128)S(1)}, f32[1,2,1536]{2,1,0:T(2,128)}, u32[]{:S(2)}) copy-start(f32[1,2,1536]{2,1,0:T(2,128)} %param.16) | copy-start | bytes 36868
  11.5 14.6 %copy-start.19 = (f32[1,2,1536]{2,1,0:T(2,128)S(1)}, f32[1,2,1536]{2,1,0:T(2,128)}, u32[]{:S(2)}) copy-start(f32[1,2,1536]{2,1,0:T(2,128)} %param.14) | copy-start | bytes 36868
  11.5 97.7 %all-to-all-start = ((bf16[32,6,8,1536]{3,2,1,0:T(8,128)(2,1)}), bf16[32,6,8,1536]{3,2,1,0:T(8,128)(2,1)}, u32[]{:S(2)}, u32[]{:S(2)}) async-start(bf16[32,6,8,1536]{3,2,1,0:T(8,128)(2,1)} %stack.8), calls=%async_computation | async-start | bytes 9437184 | tf_op jit(solution)/shard_map/all_to_all | solution.py:55
  111.9 3.1 %copy-start = (bf16[32,6,8,1536]{3,2,0,1:T(8,128)(2,1)}, bf16[32,6,8,1536]{3,2,0,1:T(8,128)(2,1)S(1)}, u32[]{:S(2)}) copy-start(bf16[32,6,8,1536]{3,2,0,1:T(8,128)(2,1)S(1)} %copy.122) | copy-start | bytes 14155780
  117.6 4.9 %copy-start.4 = (bf16[256,12,128]{2,0,1:T(8,128)(2,1)}, bf16[256,12,128]{2,0,1:T(8,128)(2,1)S(1)}, u32[]{:S(2)}) copy-start(bf16[256,12,128]{2,0,1:T(8,128)(2,1)S(1)} %fusion.17) | copy-start | bytes 2359300
  122.3 1.1 copy-start.12
  123.5 1.5 copy-start.13
  130.6 4.8 %copy-start.8 = (bf16[1,32,8,1536]{3,2,1,0:T(8,128)(2,1)S(1)}, bf16[1,32,8,1536]{3,2,1,0:T(8,128)(2,1)}, u32[]{:S(2)}) copy-start(bf16[1,32,8,1536]{3,2,1,0:T(8,128)(2,1)} %get-tuple-element.24) | copy-start | bytes 2359300
  146.9 3.0 %copy-start.9 = (bf16[256,12,128]{2,0,1:T(8,128)(2,1)}, bf16[256,12,128]{2,0,1:T(8,128)(2,1)S(1)}, u32[]{:S(2)}) copy-start(bf16[256,12,128]{2,0,1:T(8,128)(2,1)S(1)} %get-tuple-element.21) | copy-start | bytes 2359300
  148.4 1.4 copy-start.6
  148.4 1.4 copy-start.11
  152.2 2.0 copy-start.3
  156.7 47.2 %collective-permute-start = (bf16[256,1536]{1,0:T(8,128)(2,1)}, bf16[256,1536]{1,0:T(8,128)(2,1)S(1)}, u32[]{:S(2)}, u32[]{:S(2)}) collective-permute-start(bf16[256,1536]{1,0:T(8,128)(2,1)} %fusion.66), channel_id=1, source_target_pairs={{0,32},{32,64},{64,96},{96,128},{128,160},{160,192},{192,224},{224... | collective-permute-start | bytes 2359304 | tf_op jit(solution)/shard_map/ppermute | solution.py:104
  216.0 1.4 copy-start.1
  216.1 1.7 copy-start.5
  217.9 1.5 copy-start.14
  217.9 1.5 copy-start.15
  233.5 1.4 copy-start.2
  233.6 1.7 copy-start.7
  235.4 1.3 copy-start.10
